TPU v7x, 256 devices: a whole 4x4x8 slice. The times are simulated.
256 devices in a mesh: grp: 4 (over x), tok: 8 (over z), mdl: 8 (over y, core).
Axes of the slice: x: 4, y: 4, z: 8, core: 2. Of those that a mesh axis runs over, the one named last changes fastest.
Arguments:
- hidden_in: bfloat16 [4, 1024, 5120], P('grp', 'tok', 'mdl'), may hold values from -8 to 8
- seg_ids: int32 [4, 1024], replicated, may hold values from 0 to 3, never falling along the last dimension, each value on 1 to 768 neighbouring positions
- request_prefix: int32 [4, 4], replicated, may hold values from 0 to 1
- page_table: int32 [32], replicated, may hold values from 0 to 31, each once
- prefix_cache: bfloat16 [32, 256, 8, 256], P(('grp', 'mdl'), None, 'tok'), may hold values from -200 to 200
- attn_gain: float32 [5120], P('mdl'), may hold values from 0.1 to 1.9
- w_query: bfloat16 [5120, 5120], P('mdl', 'tok'), may hold values from -0.078125 to 0.078125
- w_key: bfloat16 [5120, 1024], P('mdl', 'tok'), may hold values from -0.25 to 0.25
- w_value: bfloat16 [5120, 1024], P('mdl', 'tok'), may hold values from -0.078125 to 0.078125
- w_out: bfloat16 [5120, 5120], P('tok', 'mdl'), may hold values from -0.078125 to 0.078125
- ffn_gain: float32 [5120], P('mdl'), may hold values from 0.1 to 1.9
- w_gate: bfloat16 [5120, 14336], P('mdl', 'tok'), may hold values from -0.078125 to 0.078125
- w_up: bfloat16 [5120, 14336], P('mdl', 'tok'), may hold values from -0.078125 to 0.078125
- w_down: bfloat16 [14336, 5120], P('tok', 'mdl'), may hold values from -0.046875 to 0.046875
- final_gain: float32 [5120], replicated, may hold values from 0.1 to 1.9
- lm_head: bfloat16 [76800, 5120], P(('grp', 'tok', 'mdl')), may hold values from -0.25 to 0.25
Outputs:
- hidden_out: bfloat16 [4, 1024, 5120], P('grp', 'tok', 'mdl')
- new_kv: bfloat16 [4, 1024, 8, 256], P('grp', 'mdl', 'tok')
- req_norm: float32 [4, 4], P('grp')
- max_logit: float32 [4, 4], replicated
- logits: float32 [16, 76800], P(None, ('grp', 'tok', 'mdl'))
Inputs may be any that keep to these rules, and one draw needn't show every extreme that they name: `seg_ids`: requests of a group are contiguous, in order, and none is empty. `page_table`: each physical slot holds exactly one logical page.
All inputs are finite; a program needn't handle non-finite values.
Results may differ from a plain program's by a relative error of at most 0.024.
Values may be sent and summed in bfloat16 or wider, within the bound.
No kernel may reach another device: no remote copies, remote signals or barrier semaphores. Data moves between devices by JAX's collectives and lax.ppermute only.
A program may use at most 128 MiB of HBM per device.

v0:
```python
import jax
import jax.numpy as jnp
from jax import lax
from jax.sharding import PartitionSpec as P

PREFIX = 4096
PAGE = 256
EPS = 1e-06
THETA = 1000000.0
NEG = -1e30


def rotate(tensor, positions):
    half_dim = tensor.shape[-1] // 2
    frequency = THETA ** (-(jnp.arange(half_dim, dtype=jnp.float32) * 2.0 / tensor.shape[-1]))
    angles = positions.astype(jnp.float32)[:, None] * frequency[None, :]
    cosine = jnp.cos(angles)[:, None, :]
    sine_part = jnp.sin(angles)[:, None, :]
    first_part = tensor[..., :half_dim]
    second = tensor[..., half_dim:]
    return jnp.concatenate(
        [first_part * cosine - second * sine_part, second * cosine + first_part * sine_part], -1
    )


def on_device(
    hidden_in,
    seg_ids,
    request_prefix,
    page_table,
    prefix_cache,
    attn_gain,
    w_query,
    w_key,
    w_value,
    w_out,
    ffn_gain,
    w_gate,
    w_up,
    w_down,
    final_gain,
    lm_head,
):
    groups_total = seg_ids.shape[0]
    seq_len = seg_ids.shape[1]
    req_count = request_prefix.shape[1]
    tok_rows = hidden_in.shape[1]
    feat_dev = hidden_in.shape[2]
    model_width = feat_dev * lax.axis_size("mdl")
    head_dim = prefix_cache.shape[3] // 2
    kv_dev = prefix_cache.shape[2]
    heads_dev = w_query.shape[1] // head_dim
    group_size = heads_dev // kv_dev
    page_len = prefix_cache.shape[1]
    slot_total = page_table.shape[0]
    rows_mdl = seq_len // lax.axis_size("mdl")
    group_idx = lax.axis_index("grp")
    tok_idx = lax.axis_index("tok")
    mdl_idx = lax.axis_index("mdl")
    score_scale = head_dim ** (-0.5)
    tokens = hidden_in[0].astype(jnp.float32)
    squares = lax.psum(jnp.sum(tokens * tokens, -1), "mdl")
    normed = (tokens * lax.rsqrt(squares[:, None] / model_width + EPS) * attn_gain).astype(
        jnp.bfloat16
    )
    w_joined = jnp.concatenate([w_query, w_key, w_value], 1)
    partial_qkv = jnp.dot(
        lax.all_gather(normed, "tok", axis=0, tiled=True),
        w_joined,
        preferred_element_type=jnp.float32,
    )
    qkv_rows = lax.psum_scatter(partial_qkv, "mdl", scatter_dimension=0, tiled=True)
    q_cols = heads_dev * head_dim
    kv_cols = kv_dev * head_dim
    queries = qkv_rows[:, :q_cols].reshape(rows_mdl, heads_dev, head_dim)
    key_rows = qkv_rows[:, q_cols : q_cols + kv_cols].reshape(rows_mdl, kv_dev, head_dim)
    value_rows = qkv_rows[:, q_cols + kv_cols :].reshape(rows_mdl, kv_dev, head_dim)
    seg_row = lax.dynamic_index_in_dim(seg_ids, group_idx, 0, keepdims=False)
    prefix_row = lax.dynamic_index_in_dim(request_prefix, group_idx, 0, keepdims=False)
    requests = jnp.arange(req_count, dtype=jnp.int32)
    member = seg_row[:, None] == requests[None, :]
    counts = jnp.sum(member.astype(jnp.int32), 0)
    offsets = jnp.cumsum(counts) - counts
    row_start = mdl_idx * rows_mdl
    my_rows = row_start + jnp.arange(rows_mdl, dtype=jnp.int32)
    my_seg = lax.dynamic_slice_in_dim(seg_row, row_start, rows_mdl)
    my_member = my_seg[:, None] == requests[None, :]
    positions = PREFIX + my_rows - jnp.sum(jnp.where(my_member, offsets[None, :], 0), 1)
    my_prefix = jnp.sum(jnp.where(my_member, prefix_row[None, :], 0), 1)
    q_rot = (
        rotate(queries, positions)
        .astype(jnp.bfloat16)
        .reshape(rows_mdl, kv_dev, group_size, head_dim)
    )
    k_rot = rotate(key_rows, positions).astype(jnp.bfloat16)
    appended = jnp.concatenate([k_rot, value_rows.astype(jnp.bfloat16)], -1)
    suffix = lax.all_gather(appended, "mdl", axis=0, tiled=True)
    every_row = jnp.arange(seq_len, dtype=jnp.int32)
    suffix_ok = ((seg_row[None, :] == my_seg[:, None]) & (every_row[None, :] <= my_rows[:, None]))[
        :, None, None, :
    ]
    suffix_scores = (
        jnp.einsum(
            "rcgd,tcd->rcgt", q_rot, suffix[..., :head_dim], preferred_element_type=jnp.float32
        )
        * score_scale
    )
    suffix_scores = jnp.where(suffix_ok, suffix_scores, NEG)
    row_max = jnp.max(suffix_scores, -1)
    suffix_weights = jnp.where(suffix_ok, jnp.exp(suffix_scores - row_max[..., None]), 0.0)
    row_total = jnp.sum(suffix_weights, -1)
    mixed = jnp.einsum(
        "rcgt,tcd->rcgd",
        suffix_weights.astype(jnp.bfloat16),
        suffix[..., head_dim:],
        preferred_element_type=jnp.float32,
    )
    slot_ids = jnp.arange(slot_total, dtype=jnp.int32)
    pages_each = PREFIX // PAGE
    slot_prefix = jnp.sum(
        jnp.where(page_table[None, :] == slot_ids[:, None], (slot_ids // pages_each)[None, :], 0), 1
    )
    piece = lax.all_gather(prefix_cache, ("grp", "mdl"), axis=0, tiled=True)
    page_count = piece.shape[0]
    key_prefix = jnp.repeat(slot_prefix, page_len)
    allowed = (my_prefix[:, None] == key_prefix[None, :])[:, None, None, :]
    flat_pages = piece.reshape(page_count * page_len, kv_dev, 2 * head_dim)
    scores = (
        jnp.einsum(
            "rcgd,kcd->rcgk", q_rot, flat_pages[..., :head_dim], preferred_element_type=jnp.float32
        )
        * score_scale
    )
    scores = jnp.where(allowed, scores, NEG)
    new_max = jnp.maximum(row_max, jnp.max(scores, -1))
    factor = jnp.exp(row_max - new_max)
    page_weights = jnp.where(allowed, jnp.exp(scores - new_max[..., None]), 0.0)
    new_total = row_total * factor + jnp.sum(page_weights, -1)
    new_mixed = mixed * factor[..., None] + jnp.einsum(
        "rcgk,kcd->rcgd",
        page_weights.astype(jnp.bfloat16),
        flat_pages[..., head_dim:],
        preferred_element_type=jnp.float32,
    )
    attended = (
        (new_mixed / new_total[..., None])
        .astype(jnp.bfloat16)
        .reshape(rows_mdl, heads_dev * head_dim)
    )
    partial_out = jnp.dot(
        lax.all_gather(attended, "mdl", axis=0, tiled=True),
        w_out,
        preferred_element_type=jnp.float32,
    )
    residual = tokens + lax.psum_scatter(
        partial_out.astype(jnp.bfloat16), "tok", scatter_dimension=0, tiled=True
    ).astype(jnp.float32)
    squares_ffn = lax.psum(jnp.sum(residual * residual, -1), "mdl")
    ffn_input = (residual * lax.rsqrt(squares_ffn[:, None] / model_width + EPS) * ffn_gain).astype(
        jnp.bfloat16
    )
    w_pair = jnp.concatenate([w_gate, w_up], 1)
    ff_dev = w_gate.shape[1]
    partial_ffn = jnp.dot(
        lax.all_gather(ffn_input, "tok", axis=0, tiled=True),
        w_pair,
        preferred_element_type=jnp.float32,
    )
    summed = lax.psum_scatter(
        partial_ffn.astype(jnp.bfloat16), "mdl", scatter_dimension=0, tiled=True
    ).astype(jnp.float32)
    activated = (jax.nn.silu(summed[:, :ff_dev]) * summed[:, ff_dev:]).astype(jnp.bfloat16)
    partial_down = jnp.dot(
        lax.all_gather(activated, "mdl", axis=0, tiled=True),
        w_down,
        preferred_element_type=jnp.float32,
    )
    final_rows = residual + lax.psum_scatter(
        partial_down.astype(jnp.bfloat16), "tok", scatter_dimension=0, tiled=True
    ).astype(jnp.float32)
    tok_start = tok_idx * tok_rows
    my_tok_rows = tok_start + jnp.arange(tok_rows, dtype=jnp.int32)
    tok_seg = lax.dynamic_slice_in_dim(seg_row, tok_start, tok_rows)
    row_squares = jnp.sum(final_rows * final_rows, -1)
    req_squares = jnp.sum(
        jnp.where(tok_seg[:, None] == requests[None, :], row_squares[:, None], 0.0), 0
    )
    ends = offsets + counts - 1
    picked = ends[:, None] == my_tok_rows[None, :]
    last_part = jnp.sum(jnp.where(picked[:, :, None], final_rows[None, :, :], 0.0), 1)
    padded = jnp.zeros((groups_total * req_count, model_width), jnp.float32)
    padded = lax.dynamic_update_slice(
        padded, last_part, (group_idx * req_count, mdl_idx * feat_dev)
    )
    req_total = lax.psum(req_squares, ("tok", "mdl"))
    last_all = lax.psum(padded, ("grp", "tok", "mdl"))
    req_norm = jnp.sqrt(req_total / (counts.astype(jnp.float32) * model_width) + EPS)
    last_normed = (
        last_all * lax.rsqrt(jnp.mean(last_all * last_all, -1, keepdims=True) + EPS) * final_gain
    ).astype(jnp.bfloat16)
    logits = lax.dot_general(
        last_normed, lm_head, (((1,), (1,)), ((), ())), preferred_element_type=jnp.float32
    )
    max_logit = lax.pmax(jnp.max(logits, -1), ("grp", "tok", "mdl")).reshape(
        groups_total, req_count
    )
    return (
        final_rows.astype(jnp.bfloat16)[None],
        appended[None],
        req_norm[None],
        max_logit,
        logits,
    )


def solution(mesh):
    return jax.shard_map(
        on_device,
        mesh=mesh,
        in_specs=(
            P("grp", "tok", "mdl"),
            P(),
            P(),
            P(),
            P(("grp", "mdl"), None, "tok", None),
            P("mdl"),
            P("mdl", "tok"),
            P("mdl", "tok"),
            P("mdl", "tok"),
            P("tok", "mdl"),
            P("mdl"),
            P("mdl", "tok"),
            P("mdl", "tok"),
            P("tok", "mdl"),
            P(),
            P(("grp", "tok", "mdl"), None),
        ),
        out_specs=(
            P("grp", "tok", "mdl"),
            P("grp", "mdl", "tok", None),
            P("grp", None),
            P(),
            P(None, ("grp", "tok", "mdl")),
        ),
        check_vma=False,
    )
```

profile of v0, /device:TPU:1, one launch (start us, length us, event | category | flops | bytes accessed | tf_op | source)
XLA Modules:
  0.0 899.1 jit_solution(10230812188905599163)
XLA Ops:
  9.2 15.0 %psum.28 = f32[128]{0:T(128)S(1)} all-reduce(f32[128]{0:T(128)S(1)} %fusion.44), channel_id=1, replica_groups=mesh['grp'=4,'tok'=8,'mdl'=8] {'mdl'}, use_global_device_ids=true, to_apply=%region_1.0 | all-reduce | flops 128 | bytes 1024 | tf_op jit(solution)/shard_map/psum | solution.py:62
  24.2 1.7 fusion.46
  26.0 35.1 %all-gather.6.cloned.1.call-done = bf16[1024,640]{1,0:T(8,128)(2,1)} async-done(((bf16[128,640]{1,0:T(8,128)(2,1)}), bf16[1024,640]{1,0:T(8,128)(2,1)}) %all-gather.6.cloned.1.call-update) | async-done | bytes 1310736 | tf_op jit(solution)/shard_map/all_gather | solution.py:68
  61.1 5.1 fusion.30
  71.6 1.6 broadcast_compare_fusion
  73.3 34.7 %reduce-scatter.5.cloned.1.call-done = f32[128,896]{0,1:T(8,128)} async-done(((f32[1024,896]{0,1:T(8,128)}), f32[128,896]{0,1:T(8,128)}) %reduce-scatter.5.cloned.1.call-update) | async-done | bytes 458768 | tf_op jit(solution)/shard_map/reduce_scatter | solution.py:72
  110.8 1.8 copy.57
  114.5 16.8 %all_gather.19 = bf16[1024,1,256]{0,2,1:T(8,128)(2,1)} all-gather(bf16[128,1,256]{0,2,1:T(8,128)(2,1)S(1)} %get-tuple-element.23), channel_id=1, replica_groups=mesh['grp'=4,'tok'=8,'mdl'=8] {'mdl'}, dimensions={0}, use_global_device_ids=true | all-gather | bytes 589824 | tf_op jit(solution)/shard_map/all_gather | solution.py:97
  131.3 1.8 subtract_convert_fusion
  133.1 12.9 %fusion = (f32[128,5]{0,1:T(8,128)S(1)}, f32[128,5,8192]{2,0,1:T(8,128)}) fusion(pred[128,8192]{1,0:T(8,128)(4,1)} %broadcast_compare_fusion, bf16[8192,1,256]{2,0,1:T(8,128)(2,1)} %bitcast.150, bf16[128,5,64]{2,0,1:T(8,128)(2,1)} %get-tuple-element.17, bf16[128,5,64]{2,0,1:T(8,128)(2,1)} %get-tuple-element.16), kind=kOutput, calls=%fused_computation.2 | convolution fusion | flops 1358232960 | bytes 24447488 | tf_op jit(solution)/shard_map/rcgd,kcd->rcgk/dot_general | solution.py:129
  146.1 2.2 fusion.10
  148.3 14.2 %fusion.21 = f32[1,128,128,5]{2,1,3,0:T(8,128)} fusion(bf16[8192,1,256]{2,0,1:T(8,128)(2,1)} %bitcast.151, f32[128,5,8192]{2,0,1:T(8,128)} %get-tuple-element.33, f32[128,5]{0,1:T(8,128)S(1)} %max.19, pred[128,8192]{1,0:T(8,128)(4,1)} %broadcast_compare_fusion), kind=kOutput, calls=%fused_computation.28 | convolution fusion | flops 1368391680 | bytes 24447488 | tf_op jit(solution)/shard_map/rcgk,kcd->rcgd/dot_general | solution.py:139
  162.5 10.7 %fusion.1 = f32[128,5]{0,1:T(8,128)S(1)} fusion(f32[128,5,8192]{2,0,1:T(8,128)} %get-tuple-element.33, f32[128,5]{0,1:T(8,128)S(1)} %max.19, pred[128,8192]{1,0:T(8,128)(4,1)} %broadcast_compare_fusion), kind=kLoop, calls=%fused_computation.3 | loop fusion | flops 26213760 | bytes 22025216 | tf_op jit(solution)/shard_map/reduce_sum | solution.py:138
  174.3 1.5 fusion.39
  175.9 27.0 %all-gather.10.cloned.1.call-done = bf16[1024,640]{0,1:T(8,128)(2,1)} async-done(((bf16[128,640]{0,1:T(8,128)(2,1)}), bf16[1024,640]{0,1:T(8,128)(2,1)}) %all-gather.10.cloned.1.call-update) | async-done | bytes 1310736 | tf_op jit(solution)/shard_map/all_gather | solution.py:151
  202.9 4.0 convolution_convert_fusion.2
  206.9 36.2 %reduce-scatter.7.cloned.1.call-done = bf16[128,640]{1,0:T(8,128)(2,1)} async-done(((bf16[1024,640]{1,0:T(8,128)(2,1)}), bf16[128,640]{1,0:T(8,128)(2,1)}) %reduce-scatter.7.cloned.1.call-update) | async-done | bytes 163856 | tf_op jit(solution)/shard_map/reduce_scatter | solution.py:155
  244.2 16.7 %psum.29 = f32[128]{0:T(128)S(1)} all-reduce(f32[128]{0:T(128)S(1)} %multiply_reduce_fusion.2), channel_id=1, replica_groups=mesh['grp'=4,'tok'=8,'mdl'=8] {'mdl'}, use_global_device_ids=true, to_apply=%region_14.15 | all-reduce | flops 128 | bytes 1024 | tf_op jit(solution)/shard_map/psum | solution.py:158
  260.9 1.7 multiply_convert_fusion.1
  262.7 30.4 %all-gather.12.cloned.1.call-done = bf16[1024,640]{1,0:T(8,128)(2,1)} async-done(((bf16[128,640]{1,0:T(8,128)(2,1)}), bf16[1024,640]{1,0:T(8,128)(2,1)}) %all-gather.12.cloned.1.call-update) | async-done | bytes 1310736 | tf_op jit(solution)/shard_map/all_gather | solution.py:165
  293.1 10.5 %convolution_convert_fusion = bf16[1024,3584]{1,0:T(8,128)(2,1)} fusion(bf16[1024,640]{1,0:T(8,128)(2,1)} %all-gather.12.cloned.1.call-done, bf16[640,1792]{1,0:T(8,128)(2,1)} %param.28, bf16[640,1792]{1,0:T(8,128)(2,1)} %param.27), kind=kOutput, calls=%fused_computation.8 | convolution fusion | flops 4710465536 | bytes 13238272 | tf_op jit(solution)/shard_map/dot_general | solution.py:164
  303.6 53.3 %reduce-scatter.9.cloned.1.call-done = bf16[128,3584]{1,0:T(8,128)(2,1)} async-done(((bf16[1024,3584]{1,0:T(8,128)(2,1)}), bf16[128,3584]{1,0:T(8,128)(2,1)}) %reduce-scatter.9.cloned.1.call-update) | async-done | bytes 917520 | tf_op jit(solution)/shard_map/reduce_scatter | solution.py:169
  356.9 1.4 convert_element_type.96
  359.4 33.1 %all-gather.14.cloned.1.call-done = bf16[1024,1792]{1,0:T(8,128)(2,1)} async-done(((bf16[128,1792]{1,0:T(8,128)(2,1)}), bf16[1024,1792]{1,0:T(8,128)(2,1)}) %all-gather.14.cloned.1.call-update) | async-done | bytes 3670032 | tf_op jit(solution)/shard_map/all_gather | solution.py:174
  392.5 6.8 convolution_convert_fusion.1
  399.5 35.1 %reduce-scatter.11.cloned.1.call-done = bf16[128,640]{1,0:T(8,128)(2,1)} async-done(((bf16[1024,640]{1,0:T(8,128)(2,1)}), bf16[128,640]{1,0:T(8,128)(2,1)}) %reduce-scatter.11.cloned.1.call-update) | async-done | bytes 163856 | tf_op jit(solution)/shard_map/reduce_scatter | solution.py:178
  434.6 1.7 multiply_reduce_fusion.1
  437.2 128.3 %psum.30 = f32[4]{0:T(128)S(1)} all-reduce(f32[4]{0:T(128)S(1)} %select_reduce_fusion.2), channel_id=1, replica_groups=mesh['grp'=4,'tok'=8,'mdl'=8] {'tok','mdl'}, use_global_device_ids=true, to_apply=%region_19.20 | all-reduce | flops 4 | bytes 32 | tf_op jit(solution)/shard_map/psum | solution.py:195
  568.2 1.7 convert_bitcast_fusion
  569.9 243.1 %all-reduce.2.cloned.1.call-done = f32[16,5120]{1,0:T(8,128)} async-done(((f32[16,5120]{1,0:T(8,128)}), f32[16,5120]{1,0:T(8,128)}) %all-reduce.2.cloned.1.call-update) | async-done | bytes 327696 | tf_op jit(solution)/shard_map/psum | solution.py:196
  814.1 2.6 fusion.72
  817.4 74.3 %pmax.7 = f32[4,4]{1,0:T(4,128)} all-reduce(f32[4,4]{1,0:T(4,128)S(1)} %reshape.445), channel_id=1, replica_groups=mesh['grp'=4,'tok'=8,'mdl'=8] {'grp','tok','mdl'}, use_global_device_ids=true, to_apply=%region_24.25 | all-reduce | flops 16 | bytes 128 | tf_op jit(solution)/shard_map/pmax | solution.py:204
  (91 shorter events, 20.3 us)
Async XLA Ops:
  8.0 806.1 %copy-start = (bf16[300,5120]{1,0:T(8,128)(2,1)S(1)}, bf16[300,5120]{1,0:T(8,128)(2,1)}, u32[]{:S(2)}) copy-start(bf16[300,5120]{1,0:T(8,128)(2,1)} %param.31) | copy-start | bytes 9216004
  8.0 53.1 %all-gather.6.cloned.1.call-start = ((), (), s32[]{:S(2)}) async-start(), calls=%async_computation.4 | async-start | bytes 1474560 | tf_op jit(solution)/shard_map/all_gather | solution.py:68
  25.9 82.0 %reduce-scatter.5.cloned.1.call-start = ((), (), s32[]{:S(2)}) async-start(), calls=%async_computation.5 | async-start | bytes 4128768 | tf_op jit(solution)/shard_map/reduce_scatter | solution.py:72
  66.2 0.7 copy-start.12
  66.3 66.8 %all-gather.8.cloned.1.call-start = ((), (), s32[]{:S(2)}) async-start(), calls=%async_computation.6 | async-start | bytes 4325376 | tf_op jit(solution)/shard_map/all_gather | solution.py:123
  66.8 136.1 %all-gather.10.cloned.1.call-start = ((), (), s32[]{:S(2)}) async-start(), calls=%async_computation.7 | async-start | bytes 1474560 | tf_op jit(solution)/shard_map/all_gather | solution.py:151
  133.1 13.0 %copy-start.5 = (bf16[1024,1,256]{0,2,1:T(8,128)(2,1)S(1)}, bf16[1024,1,256]{0,2,1:T(8,128)(2,1)}, u32[]{:S(2)}) copy-start(bf16[1024,1,256]{0,2,1:T(8,128)(2,1)} %all_gather.19) | copy-start | bytes 1572868
  133.1 13.0 %copy-start.7 = (pred[128,1024]{0,1:T(8,128)(4,1)S(1)}, pred[128,1024]{0,1:T(8,128)(4,1)}, u32[]{:S(2)}) copy-start(pred[128,1024]{0,1:T(8,128)(4,1)} %fusion.43) | copy-start | bytes 393220
  133.1 13.0 %copy-start.8 = (bf16[128,5,64]{2,0,1:T(8,128)(2,1)S(1)}, bf16[128,5,64]{2,0,1:T(8,128)(2,1)}, u32[]{:S(2)}) copy-start(bf16[128,5,64]{2,0,1:T(8,128)(2,1)} %get-tuple-element.16) | copy-start | bytes 245764
  133.1 13.0 %copy-start.9 = (bf16[128,5,64]{2,0,1:T(8,128)(2,1)S(1)}, bf16[128,5,64]{2,0,1:T(8,128)(2,1)}, u32[]{:S(2)}) copy-start(bf16[128,5,64]{2,0,1:T(8,128)(2,1)} %get-tuple-element.17) | copy-start | bytes 245764
  162.5 10.7 %copy-start.1 = (f32[1024,128,5]{1,0,2:T(8,128)S(1)}, f32[1024,128,5]{1,0,2:T(8,128)}, u32[]{:S(2)}) copy-start(f32[1024,128,5]{1,0,2:T(8,128)} %get-tuple-element.31) | copy-start | bytes 7864324
  173.2 1.0 copy-start.6
  173.2 1.1 copy-start.13
  175.8 67.4 %copy-start.2 = (bf16[1,128,640]{2,1,0:T(8,128)(2,1)S(1)}, bf16[1,128,640]{2,1,0:T(8,128)(2,1)}, u32[]{:S(2)}) copy-start(bf16[1,128,640]{2,1,0:T(8,128)(2,1)} %param.16) | copy-start | bytes 491524
  175.8 85.1 %copy-start.11 = (f32[640]{0:T(1024)S(1)}, f32[640]{0:T(1024)}, u32[]{:S(2)}) copy-start(f32[640]{0:T(1024)} %param.26) | copy-start | bytes 7684
  175.8 67.4 %reduce-scatter.7.cloned.1.call-start = ((), (), s32[]{:S(2)}) async-start(), calls=%async_computation.8 | async-start | bytes 1474560 | tf_op jit(solution)/shard_map/reduce_scatter | solution.py:155
  206.9 86.2 %all-gather.12.cloned.1.call-start = ((), (), s32[]{:S(2)}) async-start(), calls=%async_computation.9 | async-start | bytes 1474560 | tf_op jit(solution)/shard_map/all_gather | solution.py:165
  262.7 94.2 %reduce-scatter.9.cloned.1.call-start = ((), (), s32[]{:S(2)}) async-start(), calls=%async_computation.10 | async-start | bytes 8257536 | tf_op jit(solution)/shard_map/reduce_scatter | solution.py:169
  303.6 88.9 %all-gather.14.cloned.1.call-start = ((), (), s32[]{:S(2)}) async-start(), calls=%async_computation.11 | async-start | bytes 4128768 | tf_op jit(solution)/shard_map/all_gather | solution.py:174
  359.3 75.3 %copy-start.3 = (bf16[128,640]{1,0:T(8,128)(2,1)S(1)}, bf16[128,640]{1,0:T(8,128)(2,1)}, u32[]{:S(2)}) copy-start(bf16[128,640]{1,0:T(8,128)(2,1)} %reduce-scatter.7.cloned.1.call-done) | copy-start | bytes 491524
  359.3 75.3 %reduce-scatter.11.cloned.1.call-start = ((), (), s32[]{:S(2)}) async-start(), calls=%async_computation.12 | async-start | bytes 1474560 | tf_op jit(solution)/shard_map/reduce_scatter | solution.py:178
  399.3 414.8 %copy-start.10 = (f32[5120]{0:T(1024)S(1)}, f32[5120]{0:T(1024)}, u32[]{:S(2)}) copy-start(f32[5120]{0:T(1024)} %param.30) | copy-start | bytes 61444
  399.4 413.6 %all-reduce.2.cloned.1.call-start = ((), (), s32[]{:S(2)}) async-start(), calls=%async_computation.13 | async-start | bytes 655360 | tf_op jit(solution)/shard_map/psum | solution.py:196
  567.5 0.7 copy-start.4
Sparse Core Ops, SparseCore 0:
  26.1 35.0 all-gather.5
  66.4 41.5 reduce-scatter.4
  175.9 26.9 all-gather.9
  207.0 36.1 reduce-scatter.6
  262.8 30.2 all-gather.11
  303.7 53.1 reduce-scatter.8
  359.4 33.0 all-gather.13
  399.5 35.0 reduce-scatter.10
Sparse Core Ops, SparseCore 1:
  69.3 56.2 all-gather.7
  568.3 244.6 all-reduce.1
where the time goes:
time: 900 us; the launch traced here: 899 us
  waiting for transfers between devices  529 us (59%)
  blocking collectives  251 us (28%)
  matrix products  59.8 us (7%)
  other arithmetic  31.8 us (4%)
  between operations  15.8 us (2%)
  local copies, waits for them, and re-layouts  11.5 us (1%)
    psum x1, waiting for transfers between devices, on_device(): last_all = lax.psum(padded, ('grp', 'tok', 'mdl'))  243 us
    psum x1, blocking collectives, on_device(): req_total = lax.psum(req_squares, ('tok', 'mdl'))  128 us
    pmax x1, blocking collectives, on_device(): lax.pmax(jnp.max(logits, -1), ('grp', 'tok', 'mdl'))  74.3 us
    reduce_scatter x1, waiting for transfers between devices, on_device(): lax.psum_scatter(partial_ffn.astype(jnp.bfloat16), 'mdl', scatter_dimensi...  53.3 us
    reduce_scatter x1, waiting for transfers between devices, on_device(): lax.psum_scatter(partial_out.astype(jnp.bfloat16), 'tok', scatter_dimensi...  36.2 us
    all_gather x1, waiting for transfers between devices, on_device(): lax.all_gather(normed, 'tok', axis=0, tiled=True)  35.1 us
    reduce_scatter x1, waiting for transfers between devices, on_device(): lax.psum_scatter(partial_down.astype(jnp.bfloat16), 'tok', scatter_dimens...  35.1 us
    reduce_scatter x1, waiting for transfers between devices, on_device(): lax.psum_scatter(partial_qkv, 'mdl', scatter_dimension=0, tiled=True)  34.7 us
  transfers between devices with their start and end apart: 10, of which 9 were waited for; matrix products, arithmetic and copies ran while one was open for 2% of the time, Pallas kernels for 0%

commit v1 on v0

--- a/solution.py
+++ b/solution.py
@@ -8,6 +8,12 @@
 EPS = 1e-06
 THETA = 1000000.0
 NEG = -1e30
+
+
+def edges_update(vec, ax_name, at_axis):
+    z = jnp.stack([vec for _ in range(jax.lax.axis_size(ax_name))])
+    y2 = jax.lax.all_to_all(z, axis_name=ax_name, concat_axis=0, split_axis=0)
+    return jnp.concatenate(y2, axis=at_axis)
 
 
 def rotate(tensor, positions):
@@ -148,9 +154,7 @@
         .reshape(rows_mdl, heads_dev * head_dim)
     )
     partial_out = jnp.dot(
-        lax.all_gather(attended, "mdl", axis=0, tiled=True),
-        w_out,
-        preferred_element_type=jnp.float32,
+        edges_update(attended, "mdl", 0), w_out, preferred_element_type=jnp.float32
     )
     residual = tokens + lax.psum_scatter(
         partial_out.astype(jnp.bfloat16), "tok", scatter_dimension=0, tiled=True

time: 900 us -> 892 us (level)
  waiting for transfers between devices: 529 us -> 501 us
  blocking collectives: 251 us -> 273 us
    all_gather x1 -> x0, waiting for transfers between devices: 27 us -> none  [on_device(): lax.all_gather(attended, 'mdl', axis=0, tiled=True)]
    all_to_all x0 -> x1, blocking collectives: none -> 21.6 us  [edges_update(): y2 = jax.lax.all_to_all(z, axis_name=ax_name, concat_axis=0, split_axis=0)]
  transfers between devices with their start and end apart: 10 -> 9, of which waited for: 9 -> 8; matrix products, arithmetic and copies ran while one was open for 2% -> 2% of each run, Pallas kernels for 0% -> 0%
where the time goes in v1:
time: 892 us; the launch traced here: 891 us
  waiting for transfers between devices  501 us (56%)
  blocking collectives  273 us (31%)
  matrix products  57.5 us (6%)
  other arithmetic  31.8 us (4%)
  between operations  15.8 us (2%)
  local copies, waits for them, and re-layouts  11.8 us (1%)
    psum x1, waiting for transfers between devices, on_device(): last_all = lax.psum(padded, ('grp', 'tok', 'mdl'))  243 us
    psum x1, blocking collectives, on_device(): req_total = lax.psum(req_squares, ('tok', 'mdl'))  128 us
    pmax x1, blocking collectives, on_device(): lax.pmax(jnp.max(logits, -1), ('grp', 'tok', 'mdl'))  74.3 us
    reduce_scatter x1, waiting for transfers between devices, on_device(): lax.psum_scatter(partial_ffn.astype(jnp.bfloat16), 'mdl', scatter_dimensi...  53.3 us
    all_gather x1, waiting for transfers between devices, on_device(): lax.all_gather(normed, 'tok', axis=0, tiled=True)  35.1 us
    reduce_scatter x1, waiting for transfers between devices, on_device(): lax.psum_scatter(partial_out.astype(jnp.bfloat16), 'tok', scatter_dimensi...  35.1 us
    reduce_scatter x1, waiting for transfers between devices, on_device(): lax.psum_scatter(partial_down.astype(jnp.bfloat16), 'tok', scatter_dimens...  35.1 us
    reduce_scatter x1, waiting for transfers between devices, on_device(): lax.psum_scatter(partial_qkv, 'mdl', scatter_dimension=0, tiled=True)  34.7 us
  transfers between devices with their start and end apart: 9, of which 8 were waited for; matrix products, arithmetic and copies ran while one was open for 2% of the time, Pallas kernels for 0%

profile of v1, /device:TPU:1, one launch (start us, length us, event | category | flops | bytes accessed | tf_op | source)
XLA Modules:
  0.0 890.6 jit_solution(14090036110246574709)
XLA Ops:
  8.1 1.2 fusion.44
  9.2 15.0 %psum.28 = f32[128]{0:T(128)S(1)} all-reduce(f32[128]{0:T(128)S(1)} %fusion.44), channel_id=1, replica_groups=mesh['grp'=4,'tok'=8,'mdl'=8] {'mdl'}, use_global_device_ids=true, to_apply=%region_1.0 | all-reduce | flops 128 | bytes 1024 | tf_op jit(solution)/shard_map/psum | solution.py:68
  24.2 1.7 fusion.46
  26.0 35.1 %all-gather.5.cloned.1.call-done = bf16[1024,640]{1,0:T(8,128)(2,1)} async-done(((bf16[128,640]{1,0:T(8,128)(2,1)}), bf16[1024,640]{1,0:T(8,128)(2,1)}) %all-gather.5.cloned.1.call-update) | async-done | bytes 1310736 | tf_op jit(solution)/shard_map/all_gather | solution.py:74
  61.1 5.1 fusion.30
  71.6 1.6 broadcast_compare_fusion
  73.3 34.7 %reduce-scatter.5.cloned.1.call-done = f32[128,896]{0,1:T(8,128)} async-done(((f32[1024,896]{0,1:T(8,128)}), f32[128,896]{0,1:T(8,128)}) %reduce-scatter.5.cloned.1.call-update) | async-done | bytes 458768 | tf_op jit(solution)/shard_map/reduce_scatter | solution.py:78
  110.8 1.8 copy.62
  114.5 16.8 %all_gather.16 = bf16[1024,1,256]{0,2,1:T(8,128)(2,1)} all-gather(bf16[128,1,256]{0,2,1:T(8,128)(2,1)S(1)} %get-tuple-element.23), channel_id=1, replica_groups=mesh['grp'=4,'tok'=8,'mdl'=8] {'mdl'}, dimensions={0}, use_global_device_ids=true | all-gather | bytes 589824 | tf_op jit(solution)/shard_map/all_gather | solution.py:103
  131.3 1.8 subtract_convert_fusion
  133.1 12.9 %fusion = (f32[128,5]{0,1:T(8,128)S(1)}, f32[128,5,8192]{2,0,1:T(8,128)}) fusion(pred[128,8192]{1,0:T(8,128)(4,1)} %broadcast_compare_fusion, bf16[8192,1,256]{2,0,1:T(8,128)(2,1)} %bitcast.152, bf16[128,5,64]{2,0,1:T(8,128)(2,1)} %get-tuple-element.17, bf16[128,5,64]{2,0,1:T(8,128)(2,1)} %get-tuple-element.16), kind=kOutput, calls=%fused_computation.2 | convolution fusion | flops 1358232960 | bytes 24447488 | tf_op jit(solution)/shard_map/rcgd,kcd->rcgk/dot_general | solution.py:135
  146.1 2.2 fusion.10
  148.3 14.2 %fusion.21 = f32[1,128,128,5]{2,1,3,0:T(8,128)} fusion(bf16[8192,1,256]{2,0,1:T(8,128)(2,1)} %bitcast.153, f32[128,5,8192]{2,0,1:T(8,128)} %get-tuple-element.33, f32[128,5]{0,1:T(8,128)S(1)} %max.19, pred[128,8192]{1,0:T(8,128)(4,1)} %broadcast_compare_fusion), kind=kOutput, calls=%fused_computation.28 | convolution fusion | flops 1368391680 | bytes 24447488 | tf_op jit(solution)/shard_map/rcgk,kcd->rcgd/dot_general | solution.py:145
  162.5 10.7 %fusion.1 = f32[128,5]{0,1:T(8,128)S(1)} fusion(f32[128,5,8192]{2,0,1:T(8,128)} %get-tuple-element.33, f32[128,5]{0,1:T(8,128)S(1)} %max.19, pred[128,8192]{1,0:T(8,128)(4,1)} %broadcast_compare_fusion), kind=kLoop, calls=%fused_computation.3 | loop fusion | flops 26213760 | bytes 22025216 | tf_op jit(solution)/shard_map/reduce_sum | solution.py:144
  175.4 21.6 %all_to_all.5 = bf16[8,128,640]{2,1,0:T(8,128)(2,1)S(1)} all-to-all(bf16[8,128,640]{2,1,0:T(8,128)(2,1)S(1)} %stack.3), channel_id=1, replica_groups=mesh['grp'=4,'tok'=8,'mdl'=8] {'mdl'}, dimensions={0} | all-to-all | bytes 2621440 | tf_op jit(solution)/shard_map/all_to_all | solution.py:15
  197.0 2.4 convolution_convert_fusion.2
  199.5 35.1 %reduce-scatter.7.cloned.1.call-done = bf16[128,640]{1,0:T(8,128)(2,1)} async-done(((bf16[1024,640]{1,0:T(8,128)(2,1)}), bf16[128,640]{1,0:T(8,128)(2,1)}) %reduce-scatter.7.cloned.1.call-update) | async-done | bytes 163856 | tf_op jit(solution)/shard_map/reduce_scatter | solution.py:159
  235.7 16.7 %psum.29 = f32[128]{0:T(128)S(1)} all-reduce(f32[128]{0:T(128)S(1)} %multiply_reduce_fusion.2), channel_id=1, replica_groups=mesh['grp'=4,'tok'=8,'mdl'=8] {'mdl'}, use_global_device_ids=true, to_apply=%region_14.15 | all-reduce | flops 128 | bytes 1024 | tf_op jit(solution)/shard_map/psum | solution.py:162
  252.4 1.7 multiply_convert_fusion.1
  254.2 30.4 %all-gather.9.cloned.1.call-done = bf16[1024,640]{1,0:T(8,128)(2,1)} async-done(((bf16[128,640]{1,0:T(8,128)(2,1)}), bf16[1024,640]{1,0:T(8,128)(2,1)}) %all-gather.9.cloned.1.call-update) | async-done | bytes 1310736 | tf_op jit(solution)/shard_map/all_gather | solution.py:169
  284.6 10.5 %convolution_convert_fusion = bf16[1024,3584]{1,0:T(8,128)(2,1)} fusion(bf16[1024,640]{1,0:T(8,128)(2,1)} %all-gather.9.cloned.1.call-done, bf16[640,1792]{1,0:T(8,128)(2,1)} %param.28, bf16[640,1792]{1,0:T(8,128)(2,1)} %param.27), kind=kOutput, calls=%fused_computation.8 | convolution fusion | flops 4710465536 | bytes 13238272 | tf_op jit(solution)/shard_map/dot_general | solution.py:168
  295.1 53.3 %reduce-scatter.9.cloned.1.call-done = bf16[128,3584]{1,0:T(8,128)(2,1)} async-done(((bf16[1024,3584]{1,0:T(8,128)(2,1)}), bf16[128,3584]{1,0:T(8,128)(2,1)}) %reduce-scatter.9.cloned.1.call-update) | async-done | bytes 917520 | tf_op jit(solution)/shard_map/reduce_scatter | solution.py:173
  348.4 1.4 convert_element_type.96
  350.9 33.1 %all-gather.11.cloned.1.call-done = bf16[1024,1792]{1,0:T(8,128)(2,1)} async-done(((bf16[128,1792]{1,0:T(8,128)(2,1)}), bf16[1024,1792]{1,0:T(8,128)(2,1)}) %all-gather.11.cloned.1.call-update) | async-done | bytes 3670032 | tf_op jit(solution)/shard_map/all_gather | solution.py:178
  384.0 6.8 convolution_convert_fusion.1
  391.0 35.1 %reduce-scatter.11.cloned.1.call-done = bf16[128,640]{1,0:T(8,128)(2,1)} async-done(((bf16[1024,640]{1,0:T(8,128)(2,1)}), bf16[128,640]{1,0:T(8,128)(2,1)}) %reduce-scatter.11.cloned.1.call-update) | async-done | bytes 163856 | tf_op jit(solution)/shard_map/reduce_scatter | solution.py:182
  426.1 1.7 multiply_reduce_fusion.1
  428.7 128.3 %psum.30 = f32[4]{0:T(128)S(1)} all-reduce(f32[4]{0:T(128)S(1)} %select_reduce_fusion.2), channel_id=1, replica_groups=mesh['grp'=4,'tok'=8,'mdl'=8] {'tok','mdl'}, use_global_device_ids=true, to_apply=%region_19.20 | all-reduce | flops 4 | bytes 32 | tf_op jit(solution)/shard_map/psum | solution.py:199
  559.7 1.7 convert_bitcast_fusion
  561.4 243.1 %all-reduce.2.cloned.1.call-done = f32[16,5120]{1,0:T(8,128)} async-done(((f32[16,5120]{1,0:T(8,128)}), f32[16,5120]{1,0:T(8,128)}) %all-reduce.2.cloned.1.call-update) | async-done | bytes 327696 | tf_op jit(solution)/shard_map/psum | solution.py:200
  805.7 2.6 fusion.72
  808.9 74.3 %pmax.7 = f32[4,4]{1,0:T(4,128)} all-reduce(f32[4,4]{1,0:T(4,128)S(1)} %reshape.447), channel_id=1, replica_groups=mesh['grp'=4,'tok'=8,'mdl'=8] {'grp','tok','mdl'}, use_global_device_ids=true, to_apply=%region_24.25 | all-reduce | flops 16 | bytes 128 | tf_op jit(solution)/shard_map/pmax | solution.py:208
  (93 shorter events, 20.1 us)
Async XLA Ops:
  8.0 797.7 %copy-start = (bf16[300,5120]{1,0:T(8,128)(2,1)S(1)}, bf16[300,5120]{1,0:T(8,128)(2,1)}, u32[]{:S(2)}) copy-start(bf16[300,5120]{1,0:T(8,128)(2,1)} %param.31) | copy-start | bytes 9216004
  8.0 53.1 %all-gather.5.cloned.1.call-start = ((), (), s32[]{:S(2)}) async-start(), calls=%async_computation.5 | async-start | bytes 1474560 | tf_op jit(solution)/shard_map/all_gather | solution.py:74
  25.9 82.0 %reduce-scatter.5.cloned.1.call-start = ((), (), s32[]{:S(2)}) async-start(), calls=%async_computation.6 | async-start | bytes 4128768 | tf_op jit(solution)/shard_map/reduce_scatter | solution.py:78
  66.2 0.7 copy-start.13
  66.3 66.8 %all-gather.7.cloned.1.call-start = ((), (), s32[]{:S(2)}) async-start(), calls=%async_computation.7 | async-start | bytes 4325376 | tf_op jit(solution)/shard_map/all_gather | solution.py:129
  66.8 167.8 %reduce-scatter.7.cloned.1.call-start = ((), (), s32[]{:S(2)}) async-start(), calls=%async_computation.8 | async-start | bytes 1474560 | tf_op jit(solution)/shard_map/reduce_scatter | solution.py:159
  133.1 13.0 %copy-start.5 = (bf16[1024,1,256]{0,2,1:T(8,128)(2,1)S(1)}, bf16[1024,1,256]{0,2,1:T(8,128)(2,1)}, u32[]{:S(2)}) copy-start(bf16[1024,1,256]{0,2,1:T(8,128)(2,1)} %all_gather.16) | copy-start | bytes 1572868
  133.1 13.0 %copy-start.7 = (pred[128,1024]{0,1:T(8,128)(4,1)S(1)}, pred[128,1024]{0,1:T(8,128)(4,1)}, u32[]{:S(2)}) copy-start(pred[128,1024]{0,1:T(8,128)(4,1)} %fusion.43) | copy-start | bytes 393220
  133.1 13.0 %copy-start.8 = (bf16[128,5,64]{2,0,1:T(8,128)(2,1)S(1)}, bf16[128,5,64]{2,0,1:T(8,128)(2,1)}, u32[]{:S(2)}) copy-start(bf16[128,5,64]{2,0,1:T(8,128)(2,1)} %get-tuple-element.16) | copy-start | bytes 245764
  133.1 13.0 %copy-start.9 = (bf16[128,5,64]{2,0,1:T(8,128)(2,1)S(1)}, bf16[128,5,64]{2,0,1:T(8,128)(2,1)}, u32[]{:S(2)}) copy-start(bf16[128,5,64]{2,0,1:T(8,128)(2,1)} %get-tuple-element.17) | copy-start | bytes 245764
  162.5 10.7 %copy-start.1 = (f32[1024,128,5]{1,0,2:T(8,128)S(1)}, f32[1024,128,5]{1,0,2:T(8,128)}, u32[]{:S(2)}) copy-start(f32[1024,128,5]{1,0,2:T(8,128)} %get-tuple-element.31) | copy-start | bytes 7864324
  173.2 1.0 copy-start.6
  173.2 1.1 copy-start.14
  175.3 21.8 %copy-start.12 = (bf16[640,640]{1,0:T(8,128)(2,1)S(1)}, bf16[640,640]{1,0:T(8,128)(2,1)}, u32[]{:S(2)}) copy-start(bf16[640,640]{1,0:T(8,128)(2,1)} %param.25) | copy-start | bytes 2457604
  197.0 37.6 %copy-start.2 = (bf16[1,128,640]{2,1,0:T(8,128)(2,1)S(1)}, bf16[1,128,640]{2,1,0:T(8,128)(2,1)}, u32[]{:S(2)}) copy-start(bf16[1,128,640]{2,1,0:T(8,128)(2,1)} %param.16) | copy-start | bytes 491524
  197.0 55.4 %copy-start.11 = (f32[640]{0:T(1024)S(1)}, f32[640]{0:T(1024)}, u32[]{:S(2)}) copy-start(f32[640]{0:T(1024)} %param.26) | copy-start | bytes 7684
  199.4 85.2 %all-gather.9.cloned.1.call-start = ((), (), s32[]{:S(2)}) async-start(), calls=%async_computation.9 | async-start | bytes 1474560 | tf_op jit(solution)/shard_map/all_gather | solution.py:169
  254.1 94.3 %reduce-scatter.9.cloned.1.call-start = ((), (), s32[]{:S(2)}) async-start(), calls=%async_computation.10 | async-start | bytes 8257536 | tf_op jit(solution)/shard_map/reduce_scatter | solution.py:173
  295.1 88.9 %all-gather.11.cloned.1.call-start = ((), (), s32[]{:S(2)}) async-start(), calls=%async_computation.11 | async-start | bytes 4128768 | tf_op jit(solution)/shard_map/all_gather | solution.py:178
  350.8 75.3 %copy-start.3 = (bf16[128,640]{1,0:T(8,128)(2,1)S(1)}, bf16[128,640]{1,0:T(8,128)(2,1)}, u32[]{:S(2)}) copy-start(bf16[128,640]{1,0:T(8,128)(2,1)} %reduce-scatter.7.cloned.1.call-done) | copy-start | bytes 491524
  350.8 75.3 %reduce-scatter.11.cloned.1.call-start = ((), (), s32[]{:S(2)}) async-start(), calls=%async_computation.12 | async-start | bytes 1474560 | tf_op jit(solution)/shard_map/reduce_scatter | solution.py:182
  390.8 414.8 %copy-start.10 = (f32[5120]{0:T(1024)S(1)}, f32[5120]{0:T(1024)}, u32[]{:S(2)}) copy-start(f32[5120]{0:T(1024)} %param.30) | copy-start | bytes 61444
  390.9 413.6 %all-reduce.2.cloned.1.call-start = ((), (), s32[]{:S(2)}) async-start(), calls=%async_computation.13 | async-start | bytes 655360 | tf_op jit(solution)/shard_map/psum | solution.py:200
  559.0 0.7 copy-start.4
Sparse Core Ops, SparseCore 0:
  26.1 35.0 all-gather.4
  66.4 41.5 reduce-scatter.4
  199.6 35.0 reduce-scatter.6
  254.2 30.3 all-gather.8
  295.2 53.1 reduce-scatter.8
  350.9 33.0 all-gather.10
  391.0 35.0 reduce-scatter.10
Sparse Core Ops, SparseCore 1:
  69.3 56.2 all-gather.6
  559.8 244.7 all-reduce.1
